TPU v7x, 32 devices: a whole 2x2x4 slice. The times are simulated.
32 devices in a mesh: groups: 2 (over y), area: 4 (over z), neuron: 4 (over x, core).
Axes of the slice: x: 2, y: 2, z: 4, core: 2. Of those that a mesh axis runs over, the one named last changes fastest.
Arguments:
- window: bfloat16 [32, 16, 32768], P(None, 'groups', ('area', 'neuron')), parts along dimension 1, may hold values from -6 to 6
- err_grad: float32 [16, 16, 32768], P(None, 'groups', ('area', 'neuron')), parts along dimension 1, may hold values from -6 to 6
- surrogate: float32 [16, 16, 32768], P(None, 'groups', ('area', 'neuron')), parts along dimension 1, may hold values from 0 to 0.5
- lv_end: float32 [16, 32768], P('groups', ('area', 'neuron')), parts along dimension 0, may hold values from -6 to 6
- la_end: float32 [16, 32768], P('groups', ('area', 'neuron')), parts along dimension 0, may hold values from -6 to 6
- alpha: float32 [32768], P(('area', 'neuron')), may hold values from 0.8 to 0.99
- rho: float32 [32768], P(('area', 'neuron')), may hold values from 0.9 to 0.999
- beta: float32 [32768], P(('area', 'neuron')), may hold values from 0.3 to 2
- weights: bfloat16 [4, 4, 64, 4, 128, 128], P(None, 'area', 'neuron'), may hold values from -0.25 to 0.25
- block_index: int32 [4, 4, 64, 4], P(None, 'area', 'neuron'), may hold values from 0 to 63, as said below
- delays: int32 [4, 4], replicated, may hold values from 16 to 31, as said below
Outputs:
- cur_adjoint: bfloat16 [16, 16, 32768], P(None, 'groups', ('area', 'neuron')), parts along dimension 1
- lv_start: float32 [16, 32768], P('groups', ('area', 'neuron')), parts along dimension 0
- la_start: float32 [16, 32768], P('groups', ('area', 'neuron')), parts along dimension 0
There are 2 independent parts, one for each index of `groups`. A program takes and returns all parts, laid end to end along the dimension named above; an argument that names none is the same for every part. Nothing has to cross between parts.
Inputs may be any that keep to these rules, and one draw needn't show every extreme that they name: `delays`: every entry lies in 16 to 31 and both ends occur. `block_index`: both ends occur.
All inputs are finite; a program needn't handle non-finite values.
Results may differ from a plain program's by a relative error of at most 0.001.
Values may be sent and summed in bfloat16 or wider, within the bound.
No kernel may reach another device: no remote copies, remote signals or barrier semaphores. Data moves between devices by JAX's collectives and lax.ppermute only.
A program may use at most 64 MiB of HBM per device.

v0:
```python
import jax
import jax.numpy as jnp
from jax import lax
from jax.sharding import PartitionSpec as P


def partner(value, axis, bit):
    mask = 2**bit
    pairs = [(source, source ^ mask) for source in range(lax.axis_size(axis))]
    return lax.ppermute(value, axis, pairs)


def adjoint_scan(err_grad, surrogate, rec, lv_end, la_end, alpha, rho, beta):

    def step(carry, inputs):
        lv_now, la_now = carry
        error_t, surr_t, rec_t = inputs
        total = error_t + rec_t - lv_now + la_now
        lv_next = alpha * lv_now + surr_t * total
        la_next = rho * la_now - beta * surr_t * total
        return ((lv_next, la_next), lv_now.astype(jnp.bfloat16))

    (lv_start, la_start), currents = lax.scan(
        step, (lv_end, la_end), (err_grad, surrogate, rec), reverse=True
    )
    return (currents, lv_start, la_start)


def per_device(
    window, err_grad, surrogate, lv_end, la_end, alpha, rho, beta, weights, block_index, delays
):
    steps = err_grad.shape[0]
    batch = err_grad.shape[1]
    local_neurons = err_grad.shape[2]
    block_side = weights.shape[-1]
    rounds = weights.shape[0]
    levels = lax.axis_size("area").bit_length() - 1
    me_area = lax.axis_index("area")
    rec = jnp.zeros((steps * batch, local_neurons), jnp.float32)
    for rnd in range(rounds):
        bit = rnd % levels
        arrived = partner(window, "area", bit)
        start = delays[rnd, me_area] - steps
        used = lax.dynamic_slice_in_dim(arrived, start, steps, 0)
        panel = lax.all_gather(used, "neuron", axis=2, tiled=True)
        flat = panel.reshape(steps * batch, panel.shape[2] // block_side, block_side)
        picked = jnp.take(flat, block_index[rnd, 0], axis=1)
        contrib = jnp.einsum(
            "rjkc,jkcd->rjd", picked, weights[rnd, 0], preferred_element_type=jnp.float32
        )
        rec = rec + contrib.reshape(steps * batch, local_neurons)
    rec = rec.reshape(steps, batch, local_neurons)
    return adjoint_scan(err_grad, surrogate, rec, lv_end, la_end, alpha, rho, beta)


def solution(mesh):
    placed = (
        P(None, "groups", ("area", "neuron")),
        P(None, "groups", ("area", "neuron")),
        P(None, "groups", ("area", "neuron")),
        P("groups", ("area", "neuron")),
        P("groups", ("area", "neuron")),
        P(("area", "neuron")),
        P(("area", "neuron")),
        P(("area", "neuron")),
        P(None, "area", "neuron", None, None, None),
        P(None, "area", "neuron", None),
        P(),
    )
    return jax.shard_map(
        per_device,
        mesh=mesh,
        in_specs=placed,
        out_specs=(
            P(None, "groups", ("area", "neuron")),
            P("groups", ("area", "neuron")),
            P("groups", ("area", "neuron")),
        ),
        check_vma=False,
    )
```

profile of v0, /device:TPU:0, one launch (start us, length us, event | category | flops | bytes accessed | tf_op | source)
XLA Modules:
  0.0 206.2 jit_solution(3993261804340114842)
XLA Ops:
  7.2 3.1 %collective-permute-start = (bf16[32,8,2048]{2,1,0:T(8,128)(2,1)}, bf16[32,8,2048]{2,1,0:T(8,128)(2,1)S(1)}, u32[]{:S(2)}, u32[]{:S(2)}) collective-permute-start(bf16[32,8,2048]{2,1,0:T(8,128)(2,1)} %param.15), channel_id=1, source_target_pairs={{0,4},{4,0},{8,12},{12,8},{1,5},{5,1},{9,13},{13,9},{2,6},{6,2},{1... | collective-permute-start | bytes 3145736 | tf_op jit(solution)/shard_map/ppermute | solution.py:10
  10.3 1.5 constant_dynamic-slice_fusion.5
  14.4 19.3 %collective-permute-done = bf16[32,8,2048]{2,1,0:T(8,128)(2,1)S(1)} collective-permute-done((bf16[32,8,2048]{2,1,0:T(8,128)(2,1)}, bf16[32,8,2048]{2,1,0:T(8,128)(2,1)S(1)}, u32[]{:S(2)}, u32[]{:S(2)}) %collective-permute-start) | collective-permute-done | bytes 1048608 | tf_op jit(solution)/shard_map/ppermute | solution.py:10
  33.7 1.1 constant_dynamic-slice_fusion.1
  34.9 2.8 %collective-permute-start.1 = (bf16[32,8,2048]{2,1,0:T(8,128)(2,1)S(1)}, bf16[32,8,2048]{2,1,0:T(8,128)(2,1)S(1)}, u32[]{:S(2)}, u32[]{:S(2)}) collective-permute-start(bf16[32,8,2048]{2,1,0:T(8,128)(2,1)S(1)} %copy-done.12), channel_id=1, source_target_pairs={{0,8},{4,12},{8,0},{12,4},{1,9},{5,13},{9,1},{13,5},{2,10},{6,14},... | collective-permute-start | bytes 3145736 | tf_op jit(solution)/shard_map/ppermute | solution.py:10
  40.1 42.5 %collective-permute-done.1 = bf16[32,8,2048]{2,1,0:T(8,128)(2,1)S(1)} collective-permute-done((bf16[32,8,2048]{2,1,0:T(8,128)(2,1)S(1)}, bf16[32,8,2048]{2,1,0:T(8,128)(2,1)S(1)}, u32[]{:S(2)}, u32[]{:S(2)}) %collective-permute-start.1) | collective-permute-done | bytes 1048608 | tf_op jit(solution)/shard_map/ppermute | solution.py:10
  82.6 1.0 constant_dynamic-slice_fusion
  86.2 2.2 %copy.52 = bf16[16,8,64,128]{3,2,1,0:T(8,128)(2,1)S(1)} copy(bf16[16,8,64,128]{3,1,2,0:T(8,128)(2,1)} %bitcast.147) | data formatting | bytes 4194304
  88.4 1.4 copy.37
  89.8 17.6 %all-gather.7.cloned.1.call-done = bf16[16,8,8192]{2,1,0:T(8,128)(2,1)} async-done(((bf16[16,8,2048]{2,1,0:T(8,128)(2,1)}), bf16[16,8,8192]{2,1,0:T(8,128)(2,1)}) %all-gather.7.cloned.1.call-update) | async-done | bytes 2097168 | tf_op jit(solution)/shard_map/all_gather | solution.py:45
  107.4 2.2 %copy.53 = bf16[16,8,64,128]{3,2,1,0:T(8,128)(2,1)S(1)} copy(bf16[16,8,64,128]{3,1,2,0:T(8,128)(2,1)} %bitcast.148) | data formatting | bytes 4194304
  109.6 2.7 %copy.40 = bf16[128,64,128]{2,0,1:T(8,128)(2,1)} copy(bf16[128,64,128]{2,1,0:T(8,128)(2,1)S(1)} %bitcast.144) | data formatting | bytes 4194304 | tf_op jit(solution)/shard_map/reshape | solution.py:46
  112.3 19.9 %all-gather.9.cloned.1.call-done = bf16[16,8,8192]{2,1,0:T(8,128)(2,1)} async-done(((bf16[16,8,2048]{2,1,0:T(8,128)(2,1)}), bf16[16,8,8192]{2,1,0:T(8,128)(2,1)}) %all-gather.9.cloned.1.call-update) | async-done | bytes 2097168 | tf_op jit(solution)/shard_map/all_gather | solution.py:45
  132.2 2.2 %copy.54 = bf16[16,8,64,128]{3,2,1,0:T(8,128)(2,1)S(1)} copy(bf16[16,8,64,128]{3,1,2,0:T(8,128)(2,1)} %bitcast.149) | data formatting | bytes 4194304
  134.4 2.7 %copy.43 = bf16[128,64,128]{2,0,1:T(8,128)(2,1)} copy(bf16[128,64,128]{2,1,0:T(8,128)(2,1)S(1)} %bitcast.145) | data formatting | bytes 4194304 | tf_op jit(solution)/shard_map/reshape | solution.py:46
  137.1 19.1 %all-gather.11.cloned.1.call-done = bf16[16,8,8192]{2,1,0:T(8,128)(2,1)} async-done(((bf16[16,8,2048]{2,1,0:T(8,128)(2,1)}), bf16[16,8,8192]{2,1,0:T(8,128)(2,1)}) %all-gather.11.cloned.1.call-update) | async-done | bytes 2097168 | tf_op jit(solution)/shard_map/all_gather | solution.py:45
  156.2 2.2 %copy.55 = bf16[16,8,64,128]{3,2,1,0:T(8,128)(2,1)S(1)} copy(bf16[16,8,64,128]{3,1,2,0:T(8,128)(2,1)} %bitcast.150) | data formatting | bytes 4194304
  158.4 2.7 %copy.46 = bf16[128,64,128]{2,0,1:T(8,128)(2,1)} copy(bf16[128,64,128]{2,1,0:T(8,128)(2,1)S(1)} %bitcast.146) | data formatting | bytes 4194304 | tf_op jit(solution)/shard_map/reshape | solution.py:46
  161.1 2.1 %gather_fusion = bf16[64,128,128]{2,1,0:T(8,128)(2,1)} fusion(bf16[128,64,128]{2,0,1:T(8,128)(2,1)S(1)} %copy.37, s32[1024]{0:T(1024)S(1)} %pad_clamp_fusion.3), kind=kCustom, calls=%fused_computation.clone | custom fusion | bytes 4194560 | tf_op jit(solution)/shard_map/jit(_take)/gather | solution.py:47
  163.3 4.0 %gather_fusion.1 = bf16[64,128,128]{2,1,0:T(8,128)(2,1)} fusion(bf16[128,64,128]{2,0,1:T(8,128)(2,1)} %copy.40, s32[1024]{0:T(1024)S(1)} %pad_clamp_fusion.2), kind=kCustom, calls=%fused_computation.1.clone | custom fusion | bytes 4194560 | tf_op jit(solution)/shard_map/jit(_take)/gather | solution.py:47
  167.2 2.2 %gather_fusion.2 = bf16[64,128,128]{2,1,0:T(8,128)(2,1)} fusion(bf16[128,64,128]{2,0,1:T(8,128)(2,1)S(1)} %copy-done, s32[1024]{0:T(1024)S(1)} %pad_clamp_fusion.1), kind=kCustom, calls=%fused_computation.2.clone | custom fusion | bytes 4194560 | tf_op jit(solution)/shard_map/jit(_take)/gather | solution.py:47
  169.4 2.5 %gather_fusion.3 = bf16[64,128,128]{2,1,0:T(8,128)(2,1)S(1)} fusion(bf16[128,64,128]{2,0,1:T(8,128)(2,1)} %copy.46, s32[1024]{0:T(1024)S(1)} %pad_clamp_fusion), kind=kCustom, calls=%fused_computation.3.clone | custom fusion | bytes 4194560 | tf_op jit(solution)/shard_map/jit(_take)/gather | solution.py:47
  172.0 3.1 %fusion.28 = f32[16,128,128]{2,1,0:T(8,128)S(1)} fusion(bf16[4,1,16,4,128,128]{5,4,3,2,1,0:T(8,128)(2,1)} %param.23, bf16[16,4,128,128]{3,2,1,0:T(8,128)(2,1)} %bitcast.153, pred[16,4]{1,0:T(8,128)(4,1)S(1)} %copy.35), kind=kOutput, calls=%fused_computation.36 | convolution fusion | flops 269484032 | bytes 5242944 | tf_op jit(solution)/shard_map/rjkc,jkcd->rjd/dot_general | solution.py:48
  175.1 2.5 %fusion.63 = f32[16,128,128]{2,1,0:T(8,128)S(1)} fusion(f32[16,128,128]{2,1,0:T(8,128)S(1)} %fusion.28, bf16[4,1,16,4,128,128]{5,4,3,2,1,0:T(8,128)(2,1)} %param.23, bf16[16,4,128,128]{3,2,1,0:T(8,128)(2,1)S(1)} %bitcast.154, pred[16,4]{1,0:T(8,128)(4,1)S(1)} %copy.38), kind=kOutput, calls=%fused_computation.43 | convolution fusion | flops 269746176 | bytes 6291520 | tf_op jit(solution)/shard_map/rjkc,jkcd->rjd/dot_general | solution.py:48
  177.6 2.4 %fusion.58 = f32[16,128,128]{2,1,0:T(8,128)S(1)} fusion(f32[16,128,128]{2,1,0:T(8,128)S(1)} %fusion.63, bf16[4,1,16,4,128,128]{5,4,3,2,1,0:T(8,128)(2,1)} %param.23, bf16[16,4,128,128]{3,2,1,0:T(8,128)(2,1)S(1)} %bitcast.152, pred[16,4]{1,0:T(8,128)(4,1)S(1)} %copy.41), kind=kOutput, calls=%fused_computation.42 | convolution fusion | flops 269746176 | bytes 6291520 | tf_op jit(solution)/shard_map/rjkc,jkcd->rjd/dot_general | solution.py:48
  180.0 2.4 %fusion.53 = f32[128,16,128]{2,0,1:T(8,128)S(1)} fusion(f32[16,128,128]{2,1,0:T(8,128)S(1)} %fusion.58, bf16[4,1,16,4,128,128]{5,4,3,2,1,0:T(8,128)(2,1)} %param.23, bf16[16,4,128,128]{3,2,1,0:T(8,128)(2,1)S(1)} %bitcast.151, pred[16,4]{1,0:T(8,128)(4,1)S(1)} %copy.44), kind=kOutput, calls=%fused_computation.41 | convolution fusion | flops 269746176 | bytes 6291520 | tf_op jit(solution)/shard_map/rjkc,jkcd->rjd/dot_general | solution.py:48
  183.4 15.5 %while.18 = (s32[]{:T(128)}, f32[8,2048]{1,0:T(8,128)S(1)}, f32[8,2048]{1,0:T(8,128)S(1)}, bf16[16,8,2048]{2,1,0:T(8,128)(2,1)S(1)}, f32[2048]{0:T(1024)S(1)}, /...) while((s32[]{:T(128)}, f32[8,2048]{1,0:T(8,128)S(1)}, ...), condition=%wide.region_1.3_spmd, body=%wide.region_0.0_spmd.sunk | while | flops 180227 | bytes 581769 | solution.py:23
  183.4 0.9 fusion.77
  185.3 0.9 fusion.77
  187.3 0.9 fusion.77
  192.1 0.9 fusion.77
  194.0 0.9 fusion.77
  (83 shorter events, 14.7 us)
Async XLA Ops:
  7.2 27.7 %copy-start.12 = (bf16[32,8,2048]{2,1,0:T(8,128)(2,1)S(1)}, bf16[32,8,2048]{2,1,0:T(8,128)(2,1)}, u32[]{:S(2)}) copy-start(bf16[32,8,2048]{2,1,0:T(8,128)(2,1)} %param.15) | copy-start | bytes 3145732
  7.2 79.0 %all-gather.5.cloned.1.call-start = ((), (), s32[]{:S(2)}) async-start(), calls=%async_computation | async-start | bytes 2621440 | tf_op jit(solution)/shard_map/all_gather | solution.py:45
  7.2 26.5 %collective-permute-start = (bf16[32,8,2048]{2,1,0:T(8,128)(2,1)}, bf16[32,8,2048]{2,1,0:T(8,128)(2,1)S(1)}, u32[]{:S(2)}, u32[]{:S(2)}) collective-permute-start(bf16[32,8,2048]{2,1,0:T(8,128)(2,1)} %param.15), channel_id=1, source_target_pairs={{0,4},{4,0},{8,12},{12,8},{1,5},{5,1},{9,13},{13,9},{2,6},{6,2},{1... | collective-permute-start | bytes 3145736 | tf_op jit(solution)/shard_map/ppermute | solution.py:10
  34.8 50.2 %copy-start.11 = (s32[4,1,16,4]{2,3,1,0:T(4,128)S(1)}, s32[4,1,16,4]{2,3,1,0:T(4,128)}, u32[]{:S(2)}) copy-start(s32[4,1,16,4]{2,3,1,0:T(4,128)} %param.24) | copy-start | bytes 3076
  34.8 72.6 %all-gather.7.cloned.1.call-start = ((), (), s32[]{:S(2)}) async-start(), calls=%async_computation.1 | async-start | bytes 2621440 | tf_op jit(solution)/shard_map/all_gather | solution.py:45
  34.9 47.8 %collective-permute-start.1 = (bf16[32,8,2048]{2,1,0:T(8,128)(2,1)S(1)}, bf16[32,8,2048]{2,1,0:T(8,128)(2,1)S(1)}, u32[]{:S(2)}, u32[]{:S(2)}) collective-permute-start(bf16[32,8,2048]{2,1,0:T(8,128)(2,1)S(1)} %copy-done.12), channel_id=1, source_target_pairs={{0,8},{4,12},{8,0},{12,4},{1,9},{5,13},{9,1},{13,5},{2,10},{6,14},... | collective-permute-start | bytes 3145736 | tf_op jit(solution)/shard_map/ppermute | solution.py:10
  83.7 48.5 %all-gather.9.cloned.1.call-start = ((), (), s32[]{:S(2)}) async-start(), calls=%async_computation.2 | async-start | bytes 2621440 | tf_op jit(solution)/shard_map/all_gather | solution.py:45
  84.4 71.8 %all-gather.11.cloned.1.call-start = ((), (), s32[]{:S(2)}) async-start(), calls=%async_computation.3 | async-start | bytes 2621440 | tf_op jit(solution)/shard_map/all_gather | solution.py:45
  163.3 4.0 %copy-start = (bf16[128,64,128]{2,0,1:T(8,128)(2,1)S(1)}, bf16[128,64,128]{2,0,1:T(8,128)(2,1)}, u32[]{:S(2)}) copy-start(bf16[128,64,128]{2,0,1:T(8,128)(2,1)} %copy.43) | copy-start | bytes 6291460
  171.9 3.1 %copy-start.6 = (bf16[64,128,128]{2,1,0:T(8,128)(2,1)S(1)}, bf16[64,128,128]{2,1,0:T(8,128)(2,1)}, u32[]{:S(2)}) copy-start(bf16[64,128,128]{2,1,0:T(8,128)(2,1)} %gather_fusion.1) | copy-start | bytes 6291460
  175.1 2.6 %copy-start.5 = (bf16[64,128,128]{2,1,0:T(8,128)(2,1)S(1)}, bf16[64,128,128]{2,1,0:T(8,128)(2,1)}, u32[]{:S(2)}) copy-start(bf16[64,128,128]{2,1,0:T(8,128)(2,1)} %gather_fusion.2) | copy-start | bytes 6291460
  182.4 0.9 copy-start.2
  182.5 0.9 copy-start.4
  182.5 0.9 copy-start.8
  182.5 0.9 copy-start.9
  182.5 0.9 copy-start.10
  198.8 0.6 copy-start.1
  198.9 0.6 copy-start.3
  198.9 0.8 copy-start.7
Sparse Core Ops, SparseCore 0:
  34.9 23.9 all-gather.4
  83.8 23.5 all-gather.6
  109.6 22.5 all-gather.8
  133.6 22.5 all-gather.10
where the time goes:
time: 207 us; the launch traced here: 206 us
  waiting for transfers between devices  120 us (58%)
  local copies, waits for them, and re-layouts  35.4 us (17%)
  between operations  19.1 us (9%)
  other arithmetic  15.2 us (7%)
  matrix products  10.4 us (5%)
  starting transfers between devices  6.07 us (3%)
    ppermute x2, waiting for transfers between devices, partner(): return lax.ppermute(value, axis, pairs)  61.8 us
    all_gather x4, waiting for transfers between devices, per_device(): panel = lax.all_gather(used, 'neuron', axis=2, tiled=True)  56.6 us
    sub x16, other arithmetic, step(): la_next = rho * la_now - beta * surr_t * total  15 us
    gather x4, local copies, waits for them, and re-layouts, per_device(): picked = jnp.take(flat, block_index[rnd, 0], axis=1)  10.8 us
    dot_general x4, matrix products, per_device(): jnp.einsum('rjkc,jkcd->rjd', picked, weights[rnd, 0], preferred_element_t...  10.4 us
    unnamed x30, local copies, waits for them, and re-layouts  9.6 us
    reshape x4, local copies, waits for them, and re-layouts, per_device(): panel.reshape(steps * batch, panel.shape[2] // block_side, block_side)  9.53 us
    ppermute x2, starting transfers between devices, partner(): return lax.ppermute(value, axis, pairs)  5.91 us
  transfers between devices with their start and end apart: 6, of which 5 were waited for; matrix products, arithmetic and copies ran while one was open for 8% of the time, Pallas kernels for 0%

commit v1 on v0

--- a/solution.py
+++ b/solution.py
@@ -1,7 +1,26 @@
+import functools
 import jax
 import jax.numpy as jnp
 from jax import lax
 from jax.sharding import PartitionSpec as P
+
+
+def plan_counts(point, out_dim):
+    workers = lax.axis_size("neuron")
+    w_next = sorted(((b, (b + 1) % workers) for b in range(workers)))
+    answer = point
+    row_list = [answer]
+    it = 1
+    while it < workers:
+        answer = lax.ppermute(answer, axis_name="neuron", perm=w_next)
+        row_list.insert(0, answer)
+        it = it + 1
+    r_now = jnp.concatenate(row_list, axis=out_dim)
+    val2 = lax.axis_index("neuron") + 1
+    return jnp.roll(r_now, shift=val2 * point.shape[out_dim], axis=out_dim)
+
+
+show_the_body = functools.partial(plan_counts, out_dim=2)
 
 
 def partner(value, axis, bit):
@@ -42,7 +61,7 @@
         arrived = partner(window, "area", bit)
         start = delays[rnd, me_area] - steps
         used = lax.dynamic_slice_in_dim(arrived, start, steps, 0)
-        panel = lax.all_gather(used, "neuron", axis=2, tiled=True)
+        panel = show_the_body(used)
         flat = panel.reshape(steps * batch, panel.shape[2] // block_side, block_side)
         picked = jnp.take(flat, block_index[rnd, 0], axis=1)
         contrib = jnp.einsum(

time: 207 us -> 173 us (0.84)
  waiting for transfers between devices: 120 us -> 86.5 us
  other arithmetic: 15.2 us -> 31.6 us
  between operations: 19.1 us -> 6.3 us
  local copies, waits for them, and re-layouts: 35.4 us -> 28.5 us
    all_gather x4 -> x0, waiting for transfers between devices: 56.6 us -> none  [per_device(): panel = lax.all_gather(used, 'neuron', axis=2, tiled=True)]
    ppermute x0 -> x12, waiting for transfers between devices: none -> 47.4 us  [plan_counts(): answer = lax.ppermute(answer, axis_name='neuron', perm=w_next)]
    ppermute x2, waiting for transfers between devices: 61.8 us -> 39.1 us  [partner(): return lax.ppermute(value, axis, pairs)]
    unnamed x0 -> x4, other arithmetic: none -> 16.5 us
    unnamed x30 -> x40, local copies, waits for them, and re-layouts: 9.6 us -> 3.32 us
    ppermute x0 -> x12, starting transfers between devices: none -> 2.38 us  [plan_counts(): answer = lax.ppermute(answer, axis_name='neuron', perm=w_next)]
  transfers between devices with their start and end apart: 6 -> 14, of which waited for: 5 -> 10; matrix products, arithmetic and copies ran while one was open for 8% -> 14% of each run, Pallas kernels for 0% -> 0%
where the time goes in v1:
time: 173 us; the launch traced here: 172 us
  waiting for transfers between devices  86.5 us (50%)
  other arithmetic  31.6 us (18%)
  local copies, waits for them, and re-layouts  28.5 us (16%)
  matrix products  10.4 us (6%)
  starting transfers between devices  8.05 us (5%)
  between operations  6.3 us (4%)
    ppermute x12, waiting for transfers between devices, plan_counts(): answer = lax.ppermute(answer, axis_name='neuron', perm=w_next)  47.4 us
    ppermute x2, waiting for transfers between devices, partner(): return lax.ppermute(value, axis, pairs)  39.1 us
    unnamed x4, other arithmetic  16.5 us
    sub x16, other arithmetic, step(): la_next = rho * la_now - beta * surr_t * total  15 us
    gather x4, local copies, waits for them, and re-layouts, per_device(): picked = jnp.take(flat, block_index[rnd, 0], axis=1)  10.9 us
    dot_general x4, matrix products, per_device(): jnp.einsum('rjkc,jkcd->rjd', picked, weights[rnd, 0], preferred_element_t...  10.4 us
    reshape x4, local copies, waits for them, and re-layouts, per_device(): panel.reshape(steps * batch, panel.shape[2] // block_side, block_side)  9.52 us
    ppermute x2, starting transfers between devices, partner(): return lax.ppermute(value, axis, pairs)  5.68 us
  transfers between devices with their start and end apart: 14, of which 10 were waited for; matrix products, arithmetic and copies ran while one was open for 14% of the time, Pallas kernels for 0%

profile of v1, /device:TPU:0, one launch (start us, length us, event | category | flops | bytes accessed | tf_op | source)
XLA Modules:
  0.0 171.7 jit_solution(11676293428684791238)
XLA Ops:
  0.6 3.1 %collective-permute-start = (bf16[32,8,2048]{2,1,0:T(8,128)(2,1)}, bf16[32,8,2048]{2,1,0:T(8,128)(2,1)}, u32[]{:S(2)}, u32[]{:S(2)}) collective-permute-start(bf16[32,8,2048]{2,1,0:T(8,128)(2,1)} %param.17), channel_id=1, source_target_pairs={{0,4},{4,0},{8,12},{12,8},{1,5},{5,1},{9,13},{13,9},{2,6},{6,2},{1... | collective-permute-start | bytes 3145736 | tf_op jit(solution)/shard_map/ppermute | solution.py:29
  3.7 2.6 %collective-permute-start.4 = (bf16[32,8,2048]{2,1,0:T(8,128)(2,1)}, bf16[32,8,2048]{2,1,0:T(8,128)(2,1)S(1)}, u32[]{:S(2)}, u32[]{:S(2)}) collective-permute-start(bf16[32,8,2048]{2,1,0:T(8,128)(2,1)} %param.17), channel_id=1, source_target_pairs={{0,8},{4,12},{8,0},{12,4},{1,9},{5,13},{9,1},{13,5},{2,10},{6,14},... | collective-permute-start | bytes 3145736 | tf_op jit(solution)/shard_map/ppermute | solution.py:29
  6.3 1.5 constant_dynamic-slice_fusion.5
  10.4 39.1 %collective-permute-done = bf16[32,8,2048]{2,1,0:T(8,128)(2,1)} collective-permute-done((bf16[32,8,2048]{2,1,0:T(8,128)(2,1)}, bf16[32,8,2048]{2,1,0:T(8,128)(2,1)}, u32[]{:S(2)}, u32[]{:S(2)}) %collective-permute-start) | collective-permute-done | bytes 1048608 | tf_op jit(solution)/shard_map/ppermute | solution.py:29
  49.5 1.3 constant_dynamic-slice_fusion.1
  53.6 1.8 %collective-permute-start.5 = (bf16[16,8,2048]{2,1,0:T(8,128)(2,1)S(1)}, bf16[16,8,2048]{2,1,0:T(8,128)(2,1)}, u32[]{:S(2)}, u32[]{:S(2)}) collective-permute-start(bf16[16,8,2048]{2,1,0:T(8,128)(2,1)S(1)} %get-tuple-element.231), channel_id=1, source_target_pairs={{0,1},{1,2},{2,3},{3,0},{4,5},{5,6},{6,7},{7,4},{8,9},{9,10},{10,1... | collective-permute-start | bytes 1572872 | tf_op jit(solution)/shard_map/ppermute | solution.py:15
  55.9 3.7 %collective-permute-done.1 = bf16[16,8,2048]{2,1,0:T(8,128)(2,1)} collective-permute-done((bf16[16,8,2048]{2,1,0:T(8,128)(2,1)S(1)}, bf16[16,8,2048]{2,1,0:T(8,128)(2,1)}, u32[]{:S(2)}, u32[]{:S(2)}) %collective-permute-start.1) | collective-permute-done | bytes 524320 | tf_op jit(solution)/shard_map/ppermute | solution.py:15
  59.6 5.6 %collective-permute-done.5 = bf16[16,8,2048]{2,1,0:T(8,128)(2,1)} collective-permute-done((bf16[16,8,2048]{2,1,0:T(8,128)(2,1)S(1)}, bf16[16,8,2048]{2,1,0:T(8,128)(2,1)}, u32[]{:S(2)}, u32[]{:S(2)}) %collective-permute-start.5) | collective-permute-done | bytes 524320 | tf_op jit(solution)/shard_map/ppermute | solution.py:15
  65.2 5.5 %collective-permute-done.8 = bf16[16,8,2048]{2,1,0:T(8,128)(2,1)S(1)} collective-permute-done((bf16[16,8,2048]{2,1,0:T(8,128)(2,1)S(1)}, bf16[16,8,2048]{2,1,0:T(8,128)(2,1)S(1)}, u32[]{:S(2)}, u32[]{:S(2)}) %collective-permute-start.8) | collective-permute-done | bytes 524320 | tf_op jit(solution)/shard_map/ppermute | solution.py:15
  70.7 5.6 %collective-permute-done.11 = bf16[16,8,2048]{2,1,0:T(8,128)(2,1)S(1)} collective-permute-done((bf16[16,8,2048]{2,1,0:T(8,128)(2,1)S(1)}, bf16[16,8,2048]{2,1,0:T(8,128)(2,1)S(1)}, u32[]{:S(2)}, u32[]{:S(2)}) %collective-permute-start.11) | collective-permute-done | bytes 524320 | tf_op jit(solution)/shard_map/ppermute | solution.py:15
  76.3 5.7 %collective-permute-done.2 = bf16[16,8,2048]{2,1,0:T(8,128)(2,1)} collective-permute-done((bf16[16,8,2048]{2,1,0:T(8,128)(2,1)}, bf16[16,8,2048]{2,1,0:T(8,128)(2,1)}, u32[]{:S(2)}, u32[]{:S(2)}) %collective-permute-start.2) | collective-permute-done | bytes 524320 | tf_op jit(solution)/shard_map/ppermute | solution.py:15
  83.2 4.4 %collective-permute-done.6 = bf16[16,8,2048]{2,1,0:T(8,128)(2,1)} collective-permute-done((bf16[16,8,2048]{2,1,0:T(8,128)(2,1)}, bf16[16,8,2048]{2,1,0:T(8,128)(2,1)}, u32[]{:S(2)}, u32[]{:S(2)}) %collective-permute-start.6) | collective-permute-done | bytes 524320 | tf_op jit(solution)/shard_map/ppermute | solution.py:15
  87.7 5.6 %collective-permute-done.9 = bf16[16,8,2048]{2,1,0:T(8,128)(2,1)} collective-permute-done((bf16[16,8,2048]{2,1,0:T(8,128)(2,1)S(1)}, bf16[16,8,2048]{2,1,0:T(8,128)(2,1)}, u32[]{:S(2)}, u32[]{:S(2)}) %collective-permute-start.9) | collective-permute-done | bytes 524320 | tf_op jit(solution)/shard_map/ppermute | solution.py:15
  93.3 5.6 %collective-permute-done.12 = bf16[16,8,2048]{2,1,0:T(8,128)(2,1)} collective-permute-done((bf16[16,8,2048]{2,1,0:T(8,128)(2,1)S(1)}, bf16[16,8,2048]{2,1,0:T(8,128)(2,1)}, u32[]{:S(2)}, u32[]{:S(2)}) %collective-permute-start.12) | collective-permute-done | bytes 524320 | tf_op jit(solution)/shard_map/ppermute | solution.py:15
  98.9 5.6 %collective-permute-done.3 = bf16[16,8,2048]{2,1,0:T(8,128)(2,1)} collective-permute-done((bf16[16,8,2048]{2,1,0:T(8,128)(2,1)}, bf16[16,8,2048]{2,1,0:T(8,128)(2,1)}, u32[]{:S(2)}, u32[]{:S(2)}) %collective-permute-start.3) | collective-permute-done | bytes 524320 | tf_op jit(solution)/shard_map/ppermute | solution.py:15
  104.5 4.0 %fusion.32 = bf16[16,8,64,128]{3,1,2,0:T(8,128)(2,1)S(1)} fusion(s32[]{:T(128)S(6)} %select_n.57, bf16[16,8,2048]{2,1,0:T(8,128)(2,1)} %collective-permute-done.3, bf16[16,8,2048]{2,1,0:T(8,128)(2,1)} %collective-permute-done.2, bf16[16,8,2048]{2,1,0:T(8,128)(2,1)} %collective-permute-done.1, bf16[16,8,2048]{2,1,0:T(8,128)(2,1)S(1)} %get-tuple-element.233), kind=kLoop, calls=%fused_computation.72 | loop fusion | flops 16777216 | bytes 4194308
  109.2 1.4 copy.33
  110.6 4.0 %fusion.24 = bf16[16,8,64,128]{3,1,2,0:T(8,128)(2,1)S(1)} fusion(s32[]{:T(128)S(6)} %select_n.57, bf16[16,8,2048]{2,1,0:T(8,128)(2,1)S(1)} %collective-permute-done.7, bf16[16,8,2048]{2,1,0:T(8,128)(2,1)} %collective-permute-done.6, bf16[16,8,2048]{2,1,0:T(8,128)(2,1)} %collective-permute-done.5, bf16[16,8,2048]{2,1,0:T(8,128)(2,1)S(1)} %copy-done.8), kind=kLoop, calls=%fused_computation.64 | loop fusion | flops 16777216 | bytes 4194308
  115.2 2.7 %copy.36 = bf16[128,64,128]{2,0,1:T(8,128)(2,1)} copy(bf16[128,64,128]{2,1,0:T(8,128)(2,1)S(1)} %bitcast.148) | data formatting | bytes 4194304 | tf_op jit(solution)/shard_map/reshape | solution.py:65
  117.9 4.2 %fusion.16 = bf16[16,8,64,128]{3,1,2,0:T(8,128)(2,1)S(1)} fusion(s32[]{:T(128)S(6)} %select_n.57, bf16[16,8,2048]{2,1,0:T(8,128)(2,1)S(1)} %collective-permute-done.10, bf16[16,8,2048]{2,1,0:T(8,128)(2,1)} %collective-permute-done.9, bf16[16,8,2048]{2,1,0:T(8,128)(2,1)S(1)} %copy-done.12, bf16[16,8,2048]{2,1,0:T(8,128)(2,1)S(1)} %get-tuple-element.232), kind=kLoop, calls=%fused_computation.56 | loop fusion | flops 16777216 | bytes 4194308
  122.7 2.7 %copy.39 = bf16[128,64,128]{2,0,1:T(8,128)(2,1)} copy(bf16[128,64,128]{2,1,0:T(8,128)(2,1)S(1)} %bitcast.149) | data formatting | bytes 4194304 | tf_op jit(solution)/shard_map/reshape | solution.py:65
  125.4 4.3 %fusion.8 = bf16[16,8,64,128]{3,1,2,0:T(8,128)(2,1)S(1)} fusion(s32[]{:T(128)S(6)} %select_n.57, bf16[16,8,2048]{2,1,0:T(8,128)(2,1)S(1)} %collective-permute-done.13, bf16[16,8,2048]{2,1,0:T(8,128)(2,1)} %collective-permute-done.12, bf16[16,8,2048]{2,1,0:T(8,128)(2,1)S(1)} %copy-done.10, bf16[16,8,2048]{2,1,0:T(8,128)(2,1)S(1)} %get-tuple-element.230), kind=kLoop, calls=%fused_computation.48 | loop fusion | flops 16777216 | bytes 4194308
  130.4 2.7 %copy.42 = bf16[128,64,128]{2,0,1:T(8,128)(2,1)} copy(bf16[128,64,128]{2,1,0:T(8,128)(2,1)S(1)} %bitcast.150) | data formatting | bytes 4194304 | tf_op jit(solution)/shard_map/reshape | solution.py:65
  133.1 2.2 %gather_fusion = bf16[64,128,128]{2,1,0:T(8,128)(2,1)} fusion(bf16[128,64,128]{2,0,1:T(8,128)(2,1)S(1)} %copy.33, s32[1024]{0:T(1024)S(1)} %pad_clamp_fusion.3), kind=kCustom, calls=%fused_computation.clone | custom fusion | bytes 4194560 | tf_op jit(solution)/shard_map/jit(_take)/gather | solution.py:66
  135.3 3.9 %gather_fusion.1 = bf16[64,128,128]{2,1,0:T(8,128)(2,1)} fusion(bf16[128,64,128]{2,0,1:T(8,128)(2,1)} %copy.36, s32[1024]{0:T(1024)S(1)} %pad_clamp_fusion.2), kind=kCustom, calls=%fused_computation.1.clone | custom fusion | bytes 4194560 | tf_op jit(solution)/shard_map/jit(_take)/gather | solution.py:66
  139.3 2.2 %gather_fusion.2 = bf16[64,128,128]{2,1,0:T(8,128)(2,1)} fusion(bf16[128,64,128]{2,0,1:T(8,128)(2,1)S(1)} %copy-done, s32[1024]{0:T(1024)S(1)} %pad_clamp_fusion.1), kind=kCustom, calls=%fused_computation.2.clone | custom fusion | bytes 4194560 | tf_op jit(solution)/shard_map/jit(_take)/gather | solution.py:66
  141.4 2.5 %gather_fusion.3 = bf16[64,128,128]{2,1,0:T(8,128)(2,1)S(1)} fusion(bf16[128,64,128]{2,0,1:T(8,128)(2,1)} %copy.42, s32[1024]{0:T(1024)S(1)} %pad_clamp_fusion), kind=kCustom, calls=%fused_computation.3.clone | custom fusion | bytes 4194560 | tf_op jit(solution)/shard_map/jit(_take)/gather | solution.py:66
  144.0 3.1 %fusion.60 = f32[16,128,128]{2,1,0:T(8,128)S(1)} fusion(bf16[4,1,16,4,128,128]{5,4,3,2,1,0:T(8,128)(2,1)} %param.25, bf16[16,4,128,128]{3,2,1,0:T(8,128)(2,1)} %bitcast.153, pred[16,4]{1,0:T(8,128)(4,1)S(1)} %copy.31), kind=kOutput, calls=%fused_computation.100 | convolution fusion | flops 269484032 | bytes 5242944 | tf_op jit(solution)/shard_map/rjkc,jkcd->rjd/dot_general | solution.py:67
  147.1 2.5 %fusion.95 = f32[16,128,128]{2,1,0:T(8,128)S(1)} fusion(f32[16,128,128]{2,1,0:T(8,128)S(1)} %fusion.60, bf16[4,1,16,4,128,128]{5,4,3,2,1,0:T(8,128)(2,1)} %param.25, bf16[16,4,128,128]{3,2,1,0:T(8,128)(2,1)S(1)} %bitcast.154, pred[16,4]{1,0:T(8,128)(4,1)S(1)} %copy.34), kind=kOutput, calls=%fused_computation.107 | convolution fusion | flops 269746176 | bytes 6291520 | tf_op jit(solution)/shard_map/rjkc,jkcd->rjd/dot_general | solution.py:67
  149.7 2.4 %fusion.90 = f32[16,128,128]{2,1,0:T(8,128)S(1)} fusion(f32[16,128,128]{2,1,0:T(8,128)S(1)} %fusion.95, bf16[4,1,16,4,128,128]{5,4,3,2,1,0:T(8,128)(2,1)} %param.25, bf16[16,4,128,128]{3,2,1,0:T(8,128)(2,1)S(1)} %bitcast.152, pred[16,4]{1,0:T(8,128)(4,1)S(1)} %copy.37), kind=kOutput, calls=%fused_computation.106 | convolution fusion | flops 269746176 | bytes 6291520 | tf_op jit(solution)/shard_map/rjkc,jkcd->rjd/dot_general | solution.py:67
  152.1 2.4 %fusion.85 = f32[128,16,128]{2,0,1:T(8,128)S(1)} fusion(f32[16,128,128]{2,1,0:T(8,128)S(1)} %fusion.90, bf16[4,1,16,4,128,128]{5,4,3,2,1,0:T(8,128)(2,1)} %param.25, bf16[16,4,128,128]{3,2,1,0:T(8,128)(2,1)S(1)} %bitcast.151, pred[16,4]{1,0:T(8,128)(4,1)S(1)} %copy.40), kind=kOutput, calls=%fused_computation.105 | convolution fusion | flops 269746176 | bytes 6291520 | tf_op jit(solution)/shard_map/rjkc,jkcd->rjd/dot_general | solution.py:67
  155.4 15.5 %while.18 = (s32[]{:T(128)}, f32[8,2048]{1,0:T(8,128)S(1)}, f32[8,2048]{1,0:T(8,128)S(1)}, bf16[16,8,2048]{2,1,0:T(8,128)(2,1)S(1)}, f32[2048]{0:T(1024)S(1)}, /...) while((s32[]{:T(128)}, f32[8,2048]{1,0:T(8,128)S(1)}, ...), condition=%wide.region_1.4_spmd, body=%wide.region_0.3_spmd.sunk | while | flops 180227 | bytes 581777 | solution.py:42
  (109 shorter events, 21.1 us)
Async XLA Ops:
  0.6 58.9 %copy-start.17 = (s32[4,1,16,4]{2,3,1,0:T(4,128)S(1)}, s32[4,1,16,4]{2,3,1,0:T(4,128)}, u32[]{:S(2)}) copy-start(s32[4,1,16,4]{2,3,1,0:T(4,128)} %param.26) | copy-start | bytes 3076
  0.6 48.9 %collective-permute-start = (bf16[32,8,2048]{2,1,0:T(8,128)(2,1)}, bf16[32,8,2048]{2,1,0:T(8,128)(2,1)}, u32[]{:S(2)}, u32[]{:S(2)}) collective-permute-start(bf16[32,8,2048]{2,1,0:T(8,128)(2,1)} %param.17), channel_id=1, source_target_pairs={{0,4},{4,0},{8,12},{12,8},{1,5},{5,1},{9,13},{13,9},{2,6},{6,2},{1... | collective-permute-start | bytes 3145736 | tf_op jit(solution)/shard_map/ppermute | solution.py:29
  3.7 49.7 %collective-permute-start.4 = (bf16[32,8,2048]{2,1,0:T(8,128)(2,1)}, bf16[32,8,2048]{2,1,0:T(8,128)(2,1)S(1)}, u32[]{:S(2)}, u32[]{:S(2)}) collective-permute-start(bf16[32,8,2048]{2,1,0:T(8,128)(2,1)} %param.17), channel_id=1, source_target_pairs={{0,8},{4,12},{8,0},{12,4},{1,9},{5,13},{9,1},{13,5},{2,10},{6,14},... | collective-permute-start | bytes 3145736 | tf_op jit(solution)/shard_map/ppermute | solution.py:29
  50.8 8.8 %collective-permute-start.1 = (bf16[16,8,2048]{2,1,0:T(8,128)(2,1)S(1)}, bf16[16,8,2048]{2,1,0:T(8,128)(2,1)}, u32[]{:S(2)}, u32[]{:S(2)}) collective-permute-start(bf16[16,8,2048]{2,1,0:T(8,128)(2,1)S(1)} %get-tuple-element.233), channel_id=1, source_target_pairs={{0,1},{1,2},{2,3},{3,0},{4,5},{5,6},{6,7},{7,4},{8,9},{9,10},{10,1... | collective-permute-start | bytes 1572872 | tf_op jit(solution)/shard_map/ppermute | solution.py:15
  53.6 55.6 %copy-start.7 = (bf16[16,8,2048]{2,1,0:T(8,128)(2,1)}, bf16[16,8,2048]{2,1,0:T(8,128)(2,1)S(1)}, u32[]{:S(2)}) copy-start(bf16[16,8,2048]{2,1,0:T(8,128)(2,1)S(1)} %get-tuple-element.231) | copy-start | bytes 1572868
  53.6 11.6 %collective-permute-start.5 = (bf16[16,8,2048]{2,1,0:T(8,128)(2,1)S(1)}, bf16[16,8,2048]{2,1,0:T(8,128)(2,1)}, u32[]{:S(2)}, u32[]{:S(2)}) collective-permute-start(bf16[16,8,2048]{2,1,0:T(8,128)(2,1)S(1)} %get-tuple-element.231), channel_id=1, source_target_pairs={{0,1},{1,2},{2,3},{3,0},{4,5},{5,6},{6,7},{7,4},{8,9},{9,10},{10,1... | collective-permute-start | bytes 1572872 | tf_op jit(solution)/shard_map/ppermute | solution.py:15
  55.4 15.3 %collective-permute-start.8 = (bf16[16,8,2048]{2,1,0:T(8,128)(2,1)S(1)}, bf16[16,8,2048]{2,1,0:T(8,128)(2,1)S(1)}, u32[]{:S(2)}, u32[]{:S(2)}) collective-permute-start(bf16[16,8,2048]{2,1,0:T(8,128)(2,1)S(1)} %get-tuple-element.232), channel_id=1, source_target_pairs={{0,1},{1,2},{2,3},{3,0},{4,5},{5,6},{6,7},{7,4},{8,9},{9,10},{10,1... | collective-permute-start | bytes 1572872 | tf_op jit(solution)/shard_map/ppermute | solution.py:15
  55.5 20.8 %collective-permute-start.11 = (bf16[16,8,2048]{2,1,0:T(8,128)(2,1)S(1)}, bf16[16,8,2048]{2,1,0:T(8,128)(2,1)S(1)}, u32[]{:S(2)}, u32[]{:S(2)}) collective-permute-start(bf16[16,8,2048]{2,1,0:T(8,128)(2,1)S(1)} %get-tuple-element.230), channel_id=1, source_target_pairs={{0,1},{1,2},{2,3},{3,0},{4,5},{5,6},{6,7},{7,4},{8,9},{9,10},{10,1... | collective-permute-start | bytes 1572872 | tf_op jit(solution)/shard_map/ppermute | solution.py:15
  59.6 22.5 %collective-permute-start.2 = (bf16[16,8,2048]{2,1,0:T(8,128)(2,1)}, bf16[16,8,2048]{2,1,0:T(8,128)(2,1)}, u32[]{:S(2)}, u32[]{:S(2)}) collective-permute-start(bf16[16,8,2048]{2,1,0:T(8,128)(2,1)} %collective-permute-done.1), channel_id=1, source_target_pairs={{0,1},{1,2},{2,3},{3,0},{4,5},{5,6},{6,7},{7,4},{8,9},{9,10},{10,1... | collective-permute-start | bytes 1572872 | tf_op jit(solution)/shard_map/ppermute | solution.py:15
  65.2 22.5 %collective-permute-start.6 = (bf16[16,8,2048]{2,1,0:T(8,128)(2,1)}, bf16[16,8,2048]{2,1,0:T(8,128)(2,1)}, u32[]{:S(2)}, u32[]{:S(2)}) collective-permute-start(bf16[16,8,2048]{2,1,0:T(8,128)(2,1)} %collective-permute-done.5), channel_id=1, source_target_pairs={{0,1},{1,2},{2,3},{3,0},{4,5},{5,6},{6,7},{7,4},{8,9},{9,10},{10,1... | collective-permute-start | bytes 1572872 | tf_op jit(solution)/shard_map/ppermute | solution.py:15
  70.7 38.5 %copy-start.11 = (bf16[16,8,2048]{2,1,0:T(8,128)(2,1)}, bf16[16,8,2048]{2,1,0:T(8,128)(2,1)S(1)}, u32[]{:S(2)}) copy-start(bf16[16,8,2048]{2,1,0:T(8,128)(2,1)S(1)} %collective-permute-done.8) | copy-start | bytes 1572868
  70.7 22.6 %collective-permute-start.9 = (bf16[16,8,2048]{2,1,0:T(8,128)(2,1)S(1)}, bf16[16,8,2048]{2,1,0:T(8,128)(2,1)}, u32[]{:S(2)}, u32[]{:S(2)}) collective-permute-start(bf16[16,8,2048]{2,1,0:T(8,128)(2,1)S(1)} %collective-permute-done.8), channel_id=1, source_target_pairs={{0,1},{1,2},{2,3},{3,0},{4,5},{5,6},{6,7},{7,4},{8,9},{9,10},{10,1... | collective-permute-start | bytes 1572872 | tf_op jit(solution)/shard_map/ppermute | solution.py:15
  76.3 32.9 %copy-start.9 = (bf16[16,8,2048]{2,1,0:T(8,128)(2,1)}, bf16[16,8,2048]{2,1,0:T(8,128)(2,1)S(1)}, u32[]{:S(2)}) copy-start(bf16[16,8,2048]{2,1,0:T(8,128)(2,1)S(1)} %collective-permute-done.11) | copy-start | bytes 1572868
  76.3 22.6 %collective-permute-start.12 = (bf16[16,8,2048]{2,1,0:T(8,128)(2,1)S(1)}, bf16[16,8,2048]{2,1,0:T(8,128)(2,1)}, u32[]{:S(2)}, u32[]{:S(2)}) collective-permute-start(bf16[16,8,2048]{2,1,0:T(8,128)(2,1)S(1)} %collective-permute-done.11), channel_id=1, source_target_pairs={{0,1},{1,2},{2,3},{3,0},{4,5},{5,6},{6,7},{7,4},{8,9},{9,10},{10,1... | collective-permute-start | bytes 1572872 | tf_op jit(solution)/shard_map/ppermute | solution.py:15
  82.0 22.5 %collective-permute-start.3 = (bf16[16,8,2048]{2,1,0:T(8,128)(2,1)}, bf16[16,8,2048]{2,1,0:T(8,128)(2,1)}, u32[]{:S(2)}, u32[]{:S(2)}) collective-permute-start(bf16[16,8,2048]{2,1,0:T(8,128)(2,1)} %collective-permute-done.2), channel_id=1, source_target_pairs={{0,1},{1,2},{2,3},{3,0},{4,5},{5,6},{6,7},{7,4},{8,9},{9,10},{10,1... | collective-permute-start | bytes 1572872 | tf_op jit(solution)/shard_map/ppermute | solution.py:15
  87.7 22.9 %collective-permute-start.7 = (bf16[16,8,2048]{2,1,0:T(8,128)(2,1)}, bf16[16,8,2048]{2,1,0:T(8,128)(2,1)S(1)}, u32[]{:S(2)}, u32[]{:S(2)}) collective-permute-start(bf16[16,8,2048]{2,1,0:T(8,128)(2,1)} %collective-permute-done.6), channel_id=1, source_target_pairs={{0,1},{1,2},{2,3},{3,0},{4,5},{5,6},{6,7},{7,4},{8,9},{9,10},{10,1... | collective-permute-start | bytes 1572872 | tf_op jit(solution)/shard_map/ppermute | solution.py:15
  93.3 24.6 %collective-permute-start.10 = (bf16[16,8,2048]{2,1,0:T(8,128)(2,1)}, bf16[16,8,2048]{2,1,0:T(8,128)(2,1)S(1)}, u32[]{:S(2)}, u32[]{:S(2)}) collective-permute-start(bf16[16,8,2048]{2,1,0:T(8,128)(2,1)} %collective-permute-done.9), channel_id=1, source_target_pairs={{0,1},{1,2},{2,3},{3,0},{4,5},{5,6},{6,7},{7,4},{8,9},{9,10},{10,1... | collective-permute-start | bytes 1572872 | tf_op jit(solution)/shard_map/ppermute | solution.py:15
  98.9 26.5 %collective-permute-start.13 = (bf16[16,8,2048]{2,1,0:T(8,128)(2,1)}, bf16[16,8,2048]{2,1,0:T(8,128)(2,1)S(1)}, u32[]{:S(2)}, u32[]{:S(2)}) collective-permute-start(bf16[16,8,2048]{2,1,0:T(8,128)(2,1)} %collective-permute-done.12), channel_id=1, source_target_pairs={{0,1},{1,2},{2,3},{3,0},{4,5},{5,6},{6,7},{7,4},{8,9},{9,10},{10,1... | collective-permute-start | bytes 1572872 | tf_op jit(solution)/shard_map/ppermute | solution.py:15
  109.2 1.4 copy-start.8
  114.6 3.4 %copy-start.12 = (bf16[16,8,2048]{2,1,0:T(8,128)(2,1)S(1)}, bf16[16,8,2048]{2,1,0:T(8,128)(2,1)}, u32[]{:S(2)}) copy-start(bf16[16,8,2048]{2,1,0:T(8,128)(2,1)} %copy-done.11) | copy-start | bytes 1572868
  122.1 3.3 %copy-start.10 = (bf16[16,8,2048]{2,1,0:T(8,128)(2,1)S(1)}, bf16[16,8,2048]{2,1,0:T(8,128)(2,1)}, u32[]{:S(2)}) copy-start(bf16[16,8,2048]{2,1,0:T(8,128)(2,1)} %copy-done.9) | copy-start | bytes 1572868
  135.3 4.0 %copy-start = (bf16[128,64,128]{2,0,1:T(8,128)(2,1)S(1)}, bf16[128,64,128]{2,0,1:T(8,128)(2,1)}, u32[]{:S(2)}) copy-start(bf16[128,64,128]{2,0,1:T(8,128)(2,1)} %copy.39) | copy-start | bytes 6291460
  144.0 3.1 %copy-start.6 = (bf16[64,128,128]{2,1,0:T(8,128)(2,1)S(1)}, bf16[64,128,128]{2,1,0:T(8,128)(2,1)}, u32[]{:S(2)}) copy-start(bf16[64,128,128]{2,1,0:T(8,128)(2,1)} %gather_fusion.1) | copy-start | bytes 6291460
  147.1 2.6 %copy-start.5 = (bf16[64,128,128]{2,1,0:T(8,128)(2,1)S(1)}, bf16[64,128,128]{2,1,0:T(8,128)(2,1)}, u32[]{:S(2)}) copy-start(bf16[64,128,128]{2,1,0:T(8,128)(2,1)} %gather_fusion.2) | copy-start | bytes 6291460
  154.5 0.9 copy-start.2
  154.5 0.9 copy-start.4
  154.5 0.9 copy-start.14
  154.5 0.9 copy-start.15
  154.5 0.9 copy-start.16
  170.9 0.6 copy-start.1
  170.9 0.6 copy-start.3
  170.9 0.8 copy-start.13
